TPU v7x, 32 devices: a whole 2x2x4 slice. The times are simulated.
32 devices in a mesh: seq: 16 (over z, x, core), head: 2 (over y).
Axes of the slice: x: 2, y: 2, z: 4, core: 2. Of those that a mesh axis runs over, the one named last changes fastest.
Arguments:
- step_tokens: bfloat16 [2, 12, 8, 2560], P(None, None, None, 'head'), may hold values from -6 to 6
- parents: int32 [2, 12, 8], replicated, may hold values from 0 to 7
- tail_cache: bfloat16 [12, 8, 64, 2048], P(None, 'head', 'seq'), may hold values from -192 to 192
- tail_len: int32 [12], replicated, may hold values from 0 to 62, as said below
- cache: bfloat16 [8, 2048, 2048], P(None, ('seq', 'head')), may hold values from -192 to 192
- cache_len: int32 [8], replicated, may hold values from 256 to 2048, as said below
- prompt_states: bfloat16 [4, 128, 2560], P(None, 'seq', 'head'), may hold values from -6 to 6
- prompt_len: int32 [4], replicated, may hold values from 32 to 128, as said below
- in_gain: float32 [2560], P('head'), may hold values from 0.5 to 1.5
- w_query: bfloat16 [2560, 2048], P('head', 'seq'), may hold values from -0.125 to 0.125
- w_keyval: bfloat16 [2560, 2048], P('head', 'seq'), may hold values from -0.125 to 0.125
- q_gain: float32 [256], replicated, may hold values from 0.6 to 32
- k_gain: float32 [256], replicated, may hold values from 0.6 to 32
- w_out: bfloat16 [2048, 2560], P('seq', 'head'), may hold values from -0.125 to 0.125
- post_gain: float32 [2560], P('head'), may hold values from 0.5 to 1.5
- ffn_gain: float32 [2560], P('head'), may hold values from 0.5 to 1.5
- w_gate: bfloat16 [2560, 10240], P('head', 'seq'), may hold values from -0.125 to 0.125
- w_up: bfloat16 [2560, 10240], P('head', 'seq'), may hold values from -0.125 to 0.125
- w_down: bfloat16 [10240, 2560], P('seq', 'head'), may hold values from -0.0625 to 0.0625
- final_gain: float32 [2560], P('head'), may hold values from 0.5 to 1.5
Outputs:
- decoded: bfloat16 [2, 12, 8, 2560], P(None, None, None, 'head')
Inputs may be any that keep to these rules, and one draw needn't show every extreme that they name: `tail_len`: the first 4 groups have 0; the largest entry is exactly 62. `cache_len`: the largest entry is exactly 2048. `prompt_len`: the largest entry is exactly 128.
All inputs are finite; a program needn't handle non-finite values.
Results may differ from a plain program's by a relative error of at most 0.0055.
The roundings to bfloat16 on the way count: a program that leaves them out, or rounds other values in their place, can miss the bound.
Values may be sent and summed in bfloat16 or wider, within the bound.
No kernel may reach another device: no remote copies, remote signals or barrier semaphores. Data moves between devices by JAX's collectives and lax.ppermute only.
A program may use at most 128 MiB of HBM per device.

v0:
```python
import jax
import jax.numpy as jnp
from jax import lax
from jax.sharding import PartitionSpec as P

D = 2560
QH = 8
KVH = 4
HD = 256
QD = 2048
EPS = 1e-06
NEG = -1e30
QSCALE = 0.0625


def norm_heads(values, gain, scale):
    shaped = values.reshape(values.shape[:-1] + (-1, gain.shape[0]))
    shaped = shaped * lax.rsqrt(jnp.mean(shaped * shaped, -1, keepdims=True) + EPS) * gain * scale
    return shaped.reshape(values.shape)


def finish_keys(pairs, k_gain):
    half = pairs.shape[-1] // 2
    keys = norm_heads(pairs[..., :half], k_gain, 1.0)
    return jnp.concatenate([keys, pairs[..., half:]], -1).astype(jnp.bfloat16)


def split_pairs(pairs):
    half = pairs.shape[-1] // 2
    keys = pairs[..., :half].reshape(pairs.shape[:-1] + (KVH, HD))
    values = pairs[..., half:].reshape(pairs.shape[:-1] + (KVH, HD))
    return (keys, values)


def project_tokens(tokens, in_gain, w_query, w_keyval, q_gain, k_gain):
    flat = tokens.reshape(-1, tokens.shape[-1]).astype(jnp.float32)
    scaled = (flat * in_gain).astype(jnp.bfloat16)
    q_part = jnp.dot(scaled, w_query, preferred_element_type=jnp.float32)
    kv_part = jnp.dot(scaled, w_keyval, preferred_element_type=jnp.float32)
    squares = jnp.sum(flat * flat, -1)
    q_part, kv_part, squares = lax.psum((q_part, kv_part, squares), "head")
    factor = lax.rsqrt(squares / D + EPS)[:, None]
    q_raw = (q_part * factor).astype(jnp.bfloat16)
    kv_raw = (kv_part * factor).astype(jnp.bfloat16)
    block = q_raw.shape[1]
    both = lax.all_gather(jnp.concatenate([q_raw, kv_raw], 1), "seq", axis=1)
    q_raw = both[:, :, :block].reshape(both.shape[0], -1)
    kv_raw = both[:, :, block:].reshape(both.shape[0], -1)
    queries = norm_heads(q_raw.astype(jnp.float32), q_gain, QSCALE).astype(jnp.bfloat16)
    fresh = finish_keys(kv_raw.astype(jnp.float32), k_gain)
    return (queries, fresh)


def shards(
    step_tokens,
    parents,
    tail_cache,
    tail_len,
    cache,
    cache_len,
    prompt_states,
    prompt_len,
    in_gain,
    w_query,
    w_keyval,
    q_gain,
    k_gain,
    w_out,
    post_gain,
    ffn_gain,
    w_gate,
    w_up,
    w_down,
    final_gain,
):
    f32 = jnp.float32
    bf16 = jnp.bfloat16
    n_head = lax.axis_size("head")
    n_seq = lax.axis_size("seq")
    seq_at = lax.axis_index("seq")
    head_at = lax.axis_index("head")
    flat_at = seq_at * n_head + head_at
    steps, groups, beams, width = step_tokens.shape
    pre = prompt_states.shape[0]
    repeat = QH // KVH
    rows = jnp.transpose(prompt_states, (1, 0, 2)).astype(f32)
    prompt_scaled = (rows * in_gain).astype(bf16).reshape(-1, width)
    prompt_squares = jnp.sum(rows * rows, -1).reshape(-1)
    prompt_terms = jnp.dot(
        prompt_scaled,
        lax.all_gather(w_keyval, "seq", axis=1, tiled=True),
        preferred_element_type=f32,
    )
    prompt_sum, prompt_sq = (
        lax.psum_scatter(prompt_terms, "head", scatter_dimension=0, tiled=True),
        lax.psum_scatter(prompt_squares, "head", scatter_dimension=0, tiled=True),
    )
    prompt_pairs = finish_keys(prompt_sum * lax.rsqrt(prompt_sq / D + EPS)[:, None], k_gain)
    prompt_seg = prompt_pairs.shape[0] // pre
    prompt_pairs = jnp.transpose(prompt_pairs.reshape(prompt_seg, pre, -1), (1, 0, 2))
    prompt_keys, prompt_values = split_pairs(prompt_pairs)
    prompt_ok = (flat_at * prompt_seg + jnp.arange(prompt_seg))[None, :] < prompt_len[:, None]
    cache_seg = cache.shape[1]
    cache_keys, cache_values = split_pairs(cache)
    cache_ok = (flat_at * cache_seg + jnp.arange(cache_seg))[None, :] < cache_len[:, None]
    tail_seg = tail_cache.shape[2]
    local_beams = tail_cache.shape[1]
    offset = (seq_at * tail_seg + jnp.arange(tail_seg))[None, :] - tail_len[:, None]
    all_beams = jnp.arange(beams)
    every_query, every_fresh = project_tokens(
        step_tokens, in_gain, w_query, w_keyval, q_gain, k_gain
    )
    every_query = every_query.reshape(steps, groups, beams, -1)
    every_fresh = every_fresh.reshape(steps, groups, beams, -1)
    everyone = lax.all_gather(tail_cache, "head", axis=1, tiled=True)
    local_ids = head_at * local_beams + jnp.arange(local_beams)
    n_dev = n_seq * n_head
    owner = jnp.broadcast_to(all_beams[None, :, None], (groups, beams, tail_seg))
    source = jnp.broadcast_to(all_beams[None, :], (groups, beams))
    ancestors = []
    shaped_all, scores_all, tails_all = ([], [], [])
    for step in range(steps):
        link = parents[step]
        source = jnp.take_along_axis(source, link, axis=1)
        ancestors = [jnp.take_along_axis(a, link, axis=1) for a in ancestors]
        ancestors.append(jnp.broadcast_to(all_beams[None, :], (groups, beams)))
        picks = lax.dynamic_slice_in_dim(source, head_at * local_beams, local_beams, 1)
        tail_state = jnp.take_along_axis(everyone, picks[:, :, None, None], axis=1)
        for back, anc in enumerate(ancestors):
            mine = lax.dynamic_slice_in_dim(anc, head_at * local_beams, local_beams, 1)
            written = jnp.take_along_axis(every_fresh[back], mine[:, :, None], axis=1)
            tail_state = jnp.where(
                (offset == back)[:, None, :, None], written[:, :, None, :], tail_state
            )
        tail_ok = (offset <= step)[:, None, None, :] & (
            owner[:, :, None, :] == local_ids[None, None, :, None]
        )
        shaped = every_query[step].reshape(groups, beams, KVH, repeat, HD)
        tail_keys, tail_values = split_pairs(tail_state)
        pre_scores = jnp.einsum(
            "gbkrd,gtkd->gbkrt", shaped[:pre], prompt_keys, preferred_element_type=f32
        )
        dec_scores = jnp.einsum(
            "gbkrd,gtkd->gbkrt", shaped[pre:], cache_keys, preferred_element_type=f32
        )
        tail_scores = jnp.einsum(
            "gbkrd,gctkd->gbkrct", shaped, tail_keys, preferred_element_type=f32
        )
        pre_scores = jnp.where(prompt_ok[:, None, None, None, :], pre_scores, NEG)
        dec_scores = jnp.where(cache_ok[:, None, None, None, :], dec_scores, NEG)
        tail_scores = jnp.where(tail_ok[:, :, None, None, :, :], tail_scores, NEG)
        top = jnp.concatenate([jnp.max(pre_scores, -1), jnp.max(dec_scores, -1)], 0)
        top = jnp.maximum(top, jnp.max(tail_scores, (-2, -1)))
        scores_all.append((pre_scores, dec_scores, tail_scores))
        tails_all.append((tail_ok, tail_values))
        shaped_all.append(top)
    top_all = lax.pmax(jnp.stack(shaped_all), ("seq", "head"))
    weighted_all, total_all = ([], [])
    for step in range(steps):
        pre_scores, dec_scores, tail_scores = scores_all[step]
        tail_ok, tail_values = tails_all[step]
        top = top_all[step]
        pre_mask = prompt_ok[:, None, None, None, :]
        dec_mask = cache_ok[:, None, None, None, :]
        tail_mask = tail_ok[:, :, None, None, :, :]
        pre_weights = jnp.where(pre_mask, jnp.exp(pre_scores - top[:pre, ..., None]), 0.0)
        dec_weights = jnp.where(dec_mask, jnp.exp(dec_scores - top[pre:, ..., None]), 0.0)
        tail_weights = jnp.where(tail_mask, jnp.exp(tail_scores - top[..., None, None]), 0.0)
        total = jnp.concatenate([jnp.sum(pre_weights, -1), jnp.sum(dec_weights, -1)], 0)
        total = total + jnp.sum(tail_weights, (-2, -1))
        weighted = jnp.concatenate(
            [
                jnp.einsum(
                    "gbkrt,gtkd->gbkrd",
                    pre_weights.astype(bf16),
                    prompt_values,
                    preferred_element_type=f32,
                ),
                jnp.einsum(
                    "gbkrt,gtkd->gbkrd",
                    dec_weights.astype(bf16),
                    cache_values,
                    preferred_element_type=f32,
                ),
            ],
            0,
        )
        weighted = weighted + jnp.einsum(
            "gbkrct,gctkd->gbkrd",
            tail_weights.astype(bf16),
            tail_values,
            preferred_element_type=f32,
        )
        weighted_all.append(weighted.reshape(groups * beams, -1))
        total_all.append(total.reshape(groups * beams, -1))
    weighted = jnp.concatenate(weighted_all, 0)
    total = jnp.concatenate(total_all, 0)
    rows = weighted.shape[0]
    piece = QD // n_seq
    piece_head = jnp.arange(n_seq) * piece // HD
    lanes = -(-rows // 128) * 128
    packed = jnp.concatenate(
        [
            jnp.transpose(weighted.reshape(rows, n_seq, piece), (1, 0, 2)).reshape(n_seq, -1),
            jnp.pad(jnp.transpose(total[:, piece_head]), ((0, 0), (0, lanes - rows))),
        ],
        1,
    )
    packed = lax.psum_scatter(packed, "seq", scatter_dimension=0, tiled=True)
    packed = lax.psum(packed, "head")
    share = packed[0, : rows * piece].reshape(rows, piece)
    own_total = packed[0, rows * piece : rows * piece + rows]
    attn = (share / own_total[:, None]).astype(bf16)
    partial_out = jnp.dot(attn, w_out, preferred_element_type=f32)
    per_dev = rows // n_seq
    out_proj = lax.psum_scatter(
        partial_out.reshape(n_seq, per_dev, -1), "seq", scatter_dimension=0, tiled=True
    )[0]
    out_sq = lax.psum(jnp.sum(out_proj * out_proj, -1), "head")
    x_all = step_tokens.reshape(rows, -1)
    x_f = lax.dynamic_slice_in_dim(x_all, seq_at * per_dev, per_dev, 0).astype(f32)
    state = (x_f + out_proj * lax.rsqrt(out_sq / D + EPS)[:, None] * post_gain).astype(bf16)
    state_all = lax.all_gather(state, "seq", axis=0, tiled=True)
    state_f = state_all.astype(f32)
    scaled_two = (state_f * ffn_gain).astype(bf16)
    gate_part = jnp.dot(scaled_two, w_gate, preferred_element_type=f32)
    up_part = jnp.dot(scaled_two, w_up, preferred_element_type=f32)
    gate_part, up_part, state_sq = lax.psum(
        (gate_part, up_part, jnp.sum(state_f * state_f, -1)), "head"
    )
    norm_s = lax.rsqrt(state_sq / D + EPS)[:, None]
    inner = (jax.nn.gelu(gate_part * norm_s, approximate=True) * (up_part * norm_s)).astype(bf16)
    ffn_out = lax.psum_scatter(
        jnp.dot(inner, w_down, preferred_element_type=f32).reshape(n_seq, per_dev, -1),
        "seq",
        scatter_dimension=0,
        tiled=True,
    )[0]
    ffn_sq = lax.psum(jnp.sum(ffn_out * ffn_out, -1), "head")
    result = (
        state.astype(f32) + ffn_out * lax.rsqrt(ffn_sq / D + EPS)[:, None] * final_gain
    ).astype(bf16)
    result = lax.all_gather(result, "seq", axis=0, tiled=True)
    return result.reshape(steps, groups, beams, -1)


def solution(mesh):
    return jax.shard_map(
        shards,
        mesh=mesh,
        in_specs=(
            P(None, None, None, "head"),
            P(),
            P(None, "head", "seq", None),
            P(),
            P(None, ("seq", "head"), None),
            P(),
            P(None, "seq", "head"),
            P(),
            P("head"),
            P("head", "seq"),
            P("head", "seq"),
            P(),
            P(),
            P("seq", "head"),
            P("head"),
            P("head"),
            P("head", "seq"),
            P("head", "seq"),
            P("seq", "head"),
            P("head"),
        ),
        out_specs=P(None, None, None, "head"),
        check_vma=False,
    )
```

profile of v0, /device:TPU:0, one launch (start us, length us, event | category | flops | bytes accessed | tf_op | source)
XLA Modules:
  0.0 637.6 jit_solution(13518079163312761268)
XLA Ops:
  6.6 2.2 fusion.28
  8.8 2.1 fusion.27
  12.3 5.8 all-reduce.4
  18.1 18.1 %all-reduce.21.cloned.1.call-done = (f32[192,128]{1,0:T(8,128)}, f32[192,128]{1,0:T(8,128)}) async-done(((f32[192,128]{1,0:T(8,128)}, f32[192,128]{1,0:T(8,128)}), (f32[192,128]{1,0:T(8,128)}, f32[192,128]{1,0:T(8,128)})) %all-reduce.21.cloned.1.call-update) | async-done | bytes 196624 | tf_op jit(solution)/shard_map/psum | solution.py:41
  47.3 2.7 fusion.110
  50.0 2.6 reshape.490
  52.7 1.6 reshape.487
  58.6 6.4 %all-gather.9.cloned.1.call-done = bf16[12,8,4,2048]{3,2,1,0:T(4,128)(2,1)} async-done(((bf16[12,4,4,2048]{3,2,1,0:T(4,128)(2,1)}), bf16[12,8,4,2048]{3,2,1,0:T(4,128)(2,1)}) %all-gather.9.cloned.1.call-update) | async-done | bytes 1572880 | tf_op jit(solution)/shard_map/all_gather | solution.py:115
  65.0 4.0 gather_fusion.8
  69.0 2.5 gather_fusion.3
  71.5 34.7 %all-gather.11.cloned.1.call-done = bf16[192,4096]{1,0:T(8,128)(2,1)} async-done(((bf16[192,256]{1,0:T(8,128)(2,1)}), bf16[192,4096]{1,0:T(8,128)(2,1)}) %all-gather.11.cloned.1.call-update) | async-done | bytes 1572880 | tf_op jit(solution)/shard_map/all_gather | solution.py:46
  106.2 1.8 copy.317
  112.1 1.5 mul.295
  115.2 1.6 gather_fusion.4
  116.9 1.6 gather_fusion.1
  118.5 1.6 gather_fusion.6
  122.1 2.4 select_select_fusion.1
  133.3 1.7 copy.241
  135.0 3.0 fusion.38
  138.0 2.8 copy.257
  140.8 1.7 fusion.17
  142.6 1.7 fusion.118
  144.3 1.7 fusion.120
  146.0 20.5 %all-gather.7.cloned.1.call-done = bf16[1280,2048]{1,0:T(8,128)(2,1)} async-done(((bf16[1280,128]{1,0:T(8,128)(2,1)}), bf16[1280,2048]{1,0:T(8,128)(2,1)}) %all-gather.7.cloned.1.call-update) | async-done | bytes 5242896 | tf_op jit(solution)/shard_map/all_gather | solution.py:91
  166.6 4.2 fusion.122
  174.6 6.2 reduce-scatter.4.cloned.1.call-done
  185.6 40.5 %pmax.7 = f32[2,12,8,4,2]{2,4,3,1,0:T(2,128)S(1)} all-reduce(f32[2,12,8,4,2]{2,4,3,1,0:T(2,128)S(1)} %pad_maximum_fusion.2), channel_id=1, replica_groups=mesh['seq'=16,'head'=2] {'seq','head'}, use_global_device_ids=true, to_apply=%region_17.21 | all-reduce | flops 1536 | bytes 12288 | tf_op jit(solution)/shard_map/pmax | solution.py:157
  229.1 1.7 convolution_bitcast_fusion.5
  230.8 2.3 convolution_bitcast_fusion.2
  235.5 1.6 fusion.30
  241.9 1.9 copy.263
  243.7 1.5 fusion.3
  246.3 1.8 fusion.4
  248.5 1.5 concatenate.82
  254.6 94.9 %all-reduce.15.cloned.1.call-done = f32[16,24832]{1,0:T(8,128)} async-done(((f32[16,24832]{1,0:T(8,128)}), f32[16,24832]{1,0:T(8,128)}) %all-reduce.15.cloned.1.call-update) | async-done | bytes 1589264
  349.5 2.4 constant_dynamic-slice_fusion.2
  352.0 20.5 %all-reduce.13.cloned.1.call-done = f32[1,24832]{1,0:T(1,128)} async-done(((f32[1,24832]{1,0:T(1,128)}), f32[1,24832]{1,0:T(1,128)}) %all-reduce.13.cloned.1.call-update) | async-done | bytes 99344 | tf_op jit(solution)/shard_map/psum | solution.py:210
  375.9 94.0 %all-reduce.17.cloned.1.call-done = f32[16,12,1280]{2,0,1:T(8,128)} async-done(((f32[16,12,1280]{2,0,1:T(8,128)}), f32[16,12,1280]{2,0,1:T(8,128)}) %all-reduce.17.cloned.1.call-update) | async-done | bytes 983056
  469.9 1.6 constant_dynamic-slice_fusion.1
  471.7 4.9 psum.67
  477.5 21.2 %all-gather.1 = bf16[16,12,1280]{2,1,0:T(8,128)(2,1)S(1)} all-gather(bf16[1,12,1280]{2,1,0:T(8,128)(2,1)S(1)} %fusion.108), channel_id=1, replica_groups=mesh['seq'=16,'head'=2] {'seq'}, dimensions={0}, use_global_device_ids=true | all-gather | bytes 522240 | tf_op jit(solution)/shard_map/all_gather | solution.py:223
  498.8 2.9 fusion.55
  503.3 4.9 psum.69
  508.3 31.1 %all-reduce.19.cloned.1.call-done = (f32[192,640]{1,0:T(8,128)}, f32[192,640]{1,0:T(8,128)}) async-done(((f32[192,640]{1,0:T(8,128)}, f32[192,640]{1,0:T(8,128)}), (f32[192,640]{1,0:T(8,128)}, f32[192,640]{1,0:T(8,128)})) %all-reduce.19.cloned.1.call-update) | async-done | bytes 983056 | tf_op jit(solution)/shard_map/psum | solution.py:228
  539.4 1.9 fusion.44
  542.5 59.1 %reduce-scatter.6.cloned.1.call-done = f32[1,12,1280]{2,1,0:T(8,128)} async-done(((f32[16,12,1280]{2,1,0:T(8,128)}), f32[1,12,1280]{2,1,0:T(8,128)}) %reduce-scatter.6.cloned.1.call-update) | async-done | bytes 61456 | tf_op jit(solution)/shard_map/reduce_scatter | solution.py:233
  602.6 4.9 psum.71
  608.6 21.3 %all-gather.2 = bf16[16,12,1280]{2,1,0:T(8,128)(2,1)S(1)} all-gather(bf16[1,12,1280]{2,1,0:T(8,128)(2,1)S(1)} %fusion.83), channel_id=1, replica_groups=mesh['seq'=16,'head'=2] {'seq'}, dimensions={0}, use_global_device_ids=true | all-gather | bytes 522240 | tf_op jit(solution)/shard_map/all_gather | solution.py:243
  (287 shorter events, 67.2 us)
Async XLA Ops:
  6.5 532.8 %copy-start = (bf16[640,1280]{1,0:T(8,128)(2,1)S(1)}, bf16[640,1280]{1,0:T(8,128)(2,1)}, u32[]{:S(2)}) copy-start(bf16[640,1280]{1,0:T(8,128)(2,1)} %param.44) | copy-start | bytes 4915204
  6.5 5.1 copy-start.17
  6.5 29.7 %all-reduce.21.cloned.1.call-start = ((), (), s32[]{:S(2)}) async-start(), calls=%async_computation.11 | async-start | bytes 393216 | tf_op jit(solution)/shard_map/psum | solution.py:41
  6.5 5.4 copy-start.30
  6.5 5.4 copy-start.39
  10.8 27.7 %copy-start.42 = (f32[256]{0:T(256)S(1)}, f32[256]{0:T(256)}, u32[]{:S(2)}) copy-start(f32[256]{0:T(256)} %param.38) | copy-start | bytes 3076
  10.8 27.8 %copy-start.45 = (s32[12]{0:T(128)S(1)}, s32[12]{0:T(128)}, u32[]{:S(2)}) copy-start(s32[12]{0:T(128)} %param.29) | copy-start | bytes 148
  10.9 28.6 %copy-start.43 = (f32[256]{0:T(256)S(1)}, f32[256]{0:T(256)}, u32[]{:S(2)}) copy-start(f32[256]{0:T(256)} %param.37) | copy-start | bytes 3076
  10.9 28.7 %copy-start.34 = (s32[2,12,8]{1,2,0:T(8,128)S(1)}, s32[2,12,8]{1,2,0:T(8,128)}, u32[]{:S(2)}) copy-start(s32[2,12,8]{1,2,0:T(8,128)} %param.27) | copy-start | bytes 2308
  10.9 54.1 %all-gather.9.cloned.1.call-start = ((), (), s32[]{:S(2)}) async-start(), calls=%async_computation.4 | async-start | bytes 2359296 | tf_op jit(solution)/shard_map/all_gather | solution.py:115
  11.6 94.5 %all-gather.11.cloned.1.call-start = ((), (), s32[]{:S(2)}) async-start(), calls=%async_computation.7 | async-start | bytes 1671168 | tf_op jit(solution)/shard_map/all_gather | solution.py:46
  37.9 128.7 %all-gather.7.cloned.1.call-start = ((), (), s32[]{:S(2)}) async-start(), calls=%async_computation.2 | async-start | bytes 5570560 | tf_op jit(solution)/shard_map/all_gather | solution.py:91
  38.5 142.3 %reduce-scatter.4.cloned.1.call-start = ((), (), s32[]{:S(2)}) async-start(), calls=%async_computation.3 | async-start | bytes 393216 | tf_op jit(solution)/shard_map/reduce_scatter | solution.py:95
  38.6 75.7 %copy-start.31 = (f32[1,2,4,128]{3,1,2,0:T(2,128)}, f32[1,2,4,128]{3,1,2,0:T(2,128)S(1)}, u32[]{:S(2)}) copy-start(f32[1,2,4,128]{3,1,2,0:T(2,128)S(1)} %copy.316) | copy-start | bytes 12292
  52.7 4.0 copy-start.47
  52.7 4.6 copy-start.46
  58.6 82.2 %copy-start.23 = (pred[12,8,4,4]{0,1,3,2:T(8,128)(4,1)}, pred[12,8,4,4]{0,1,3,2:T(8,128)(4,1)S(1)}, u32[]{:S(2)}) copy-start(pred[12,8,4,4]{0,1,3,2:T(8,128)(4,1)S(1)} %get-tuple-element.66) | copy-start | bytes 4612
  65.0 4.0 copy-start.9
  118.5 3.6 copy-start.5
  118.5 3.6 copy-start.38
  138.0 4.6 copy-start.1
  142.6 24.0 %copy-start.20 = (bf16[32,1280]{1,0:T(8,128)(2,1)S(1)}, bf16[32,1280]{1,0:T(8,128)(2,1)}, u32[]{:S(2)}) copy-start(bf16[32,1280]{1,0:T(8,128)(2,1)} %reshape.483) | copy-start | bytes 245764
  146.0 24.8 %copy-start.4 = (f32[12,4,4,4,8,2]{0,4,3,2,5,1:T(8,128)S(1)}, f32[12,4,4,4,8,2]{0,4,3,2,5,1:T(8,128)}, u32[]{:S(2)}) copy-start(f32[12,4,4,4,8,2]{0,4,3,2,5,1:T(8,128)} %copy.241) | copy-start | bytes 147460
  146.0 24.8 %copy-start.25 = (pred[12,8,4,4]{0,1,3,2:T(8,128)(4,1)S(1)}, pred[12,8,4,4]{0,1,3,2:T(8,128)(4,1)}, u32[]{:S(2)}) copy-start(pred[12,8,4,4]{0,1,3,2:T(8,128)(4,1)} %get-tuple-element.65) | copy-start | bytes 4612
  146.0 24.9 %copy-start.10 = (bf16[12,4,4,1024]{3,2,1,0:T(4,128)(2,1)S(1)}, bf16[12,4,4,1024]{3,2,1,0:T(4,128)(2,1)}, u32[]{:S(2)}) copy-start(bf16[12,4,4,1024]{3,2,1,0:T(4,128)(2,1)} %get-tuple-element.26) | copy-start | bytes 1179652
  170.8 10.0 %copy-start.44 = (f32[16]{0:T(128)S(1)}, f32[16]{0:T(128)}, u32[]{:S(2)}) copy-start(f32[16]{0:T(128)} %fusion.99) | copy-start | bytes 196
  170.8 178.7 %all-reduce.15.cloned.1.call-start = ((), (), s32[]{:S(2)}) async-start(), calls=%async_computation.8 | async-start | bytes 3178496
  170.9 11.2 %copy-start.32 = (f32[1,2,4,128]{3,1,2,0:T(2,128)S(1)}, f32[1,2,4,128]{3,1,2,0:T(2,128)}, u32[]{:S(2)}) copy-start(f32[1,2,4,128]{3,1,2,0:T(2,128)} %copy-done.31) | copy-start | bytes 12292
  171.9 10.4 %copy-start.41 = (pred[4,4]{1,0:T(4,128)(4,1)S(1)}, pred[4,4]{1,0:T(4,128)(4,1)}, u32[]{:S(2)}) copy-start(pred[4,4]{1,0:T(4,128)(4,1)} %broadcast_compare_fusion.1) | copy-start | bytes 52
  173.0 11.7 %copy-start.28 = (f32[8,8,4,2]{1,3,2,0:T(2,128)S(1)}, f32[8,8,4,2]{1,3,2,0:T(2,128)}, u32[]{:S(2)}) copy-start(f32[8,8,4,2]{1,3,2,0:T(2,128)} %get-tuple-element.67) | copy-start | bytes 6148
  174.6 9.0 %copy-start.29 = (bf16[32,2048]{1,0:T(8,128)(2,1)S(1)}, bf16[32,2048]{1,0:T(8,128)(2,1)}, u32[]{:S(2)}) copy-start(bf16[32,2048]{1,0:T(8,128)(2,1)} %get-tuple-element.33) | copy-start | bytes 393220
  174.6 10.1 %copy-start.21 = (f32[12,8,4,2]{1,3,2,0:T(2,128)S(1)}, f32[12,8,4,2]{1,3,2,0:T(2,128)}, u32[]{:S(2)}) copy-start(f32[12,8,4,2]{1,3,2,0:T(2,128)} %copy.258) | copy-start | bytes 9220
  182.1 48.6 %copy-start.14 = (f32[8,8,4,2,64]{4,1,3,2,0:T(8,128)S(1)}, f32[8,8,4,2,64]{4,1,3,2,0:T(8,128)}, u32[]{:S(2)}) copy-start(f32[8,8,4,2,64]{4,1,3,2,0:T(8,128)} %get-tuple-element.68) | copy-start | bytes 393220
  226.8 6.4 %copy-start.15 = (f32[8,8,4,2,64]{4,1,3,2,0:T(8,128)S(1)}, f32[8,8,4,2,64]{4,1,3,2,0:T(8,128)}, u32[]{:S(2)}) copy-start(f32[8,8,4,2,64]{4,1,3,2,0:T(8,128)} %get-tuple-element.72) | copy-start | bytes 393220
  226.8 6.4 %copy-start.37 = (pred[8,64]{1,0:T(8,128)(4,1)S(1)}, pred[8,64]{1,0:T(8,128)(4,1)}, u32[]{:S(2)}) copy-start(pred[8,64]{1,0:T(8,128)(4,1)} %broadcast_compare_fusion) | copy-start | bytes 1540
  229.1 4.5 copy-start.13
  233.6 4.2 copy-start.3
  233.6 4.2 copy-start.24
  237.1 4.8 copy-start.16
  253.3 121.2 %copy-start.19 = (bf16[128,1280]{1,0:T(8,128)(2,1)S(1)}, bf16[128,1280]{1,0:T(8,128)(2,1)}, u32[]{:S(2)}) copy-start(bf16[128,1280]{1,0:T(8,128)(2,1)} %param.39) | copy-start | bytes 983044
  253.4 119.1 %all-reduce.13.cloned.1.call-start = ((), (), s32[]{:S(2)}) async-start(), calls=%async_computation.5 | async-start | bytes 198656 | tf_op jit(solution)/shard_map/psum | solution.py:210
  351.9 118.0 %all-reduce.17.cloned.1.call-start = ((), (), s32[]{:S(2)}) async-start(), calls=%async_computation.9 | async-start | bytes 1966080
  373.2 103.4 %copy-start.35 = (f32[1280]{0:T(1024)S(1)}, f32[1280]{0:T(1024)}, u32[]{:S(2)}) copy-start(f32[1280]{0:T(1024)} %param.40) | copy-start | bytes 15364
  375.8 123.0 %copy-start.33 = (f32[1280]{0:T(1024)S(1)}, f32[1280]{0:T(1024)}, u32[]{:S(2)}) copy-start(f32[1280]{0:T(1024)} %param.41) | copy-start | bytes 15364
  375.8 163.5 %all-reduce.19.cloned.1.call-start = ((), (), s32[]{:S(2)}) async-start(), calls=%async_computation.10 | async-start | bytes 1966080 | tf_op jit(solution)/shard_map/psum | solution.py:228
  498.8 2.9 copy-start.8
  503.1 98.5 %reduce-scatter.6.cloned.1.call-start = ((), (), s32[]{:S(2)}) async-start(), calls=%async_computation.6 | async-start | bytes 1392640 | tf_op jit(solution)/shard_map/reduce_scatter | solution.py:233
  541.3 66.3 %copy-start.40 = (f32[1280]{0:T(1024)S(1)}, f32[1280]{0:T(1024)}, u32[]{:S(2)}) copy-start(f32[1280]{0:T(1024)} %param.45) | copy-start | bytes 15364
  (12 other events, 18.8 us)
Sparse Core Ops, SparseCore 0:
  11.0 25.1 all-reduce.20
  37.7 27.1 all-gather.8
  67.2 38.9 all-gather.10
  108.2 58.3 all-gather.6
  170.9 9.8 reduce-scatter.3
  253.5 95.9 all-reduce.14
  352.0 20.3 all-reduce.12
  375.9 93.9 all-reduce.16
  503.2 36.0 all-reduce.18
  543.3 58.2 reduce-scatter.5
where the time goes:
time: 639 us; the launch traced here: 638 us
  waiting for transfers between devices  387 us (61%)
  blocking collectives  104 us (16%)
  local copies, waits for them, and re-layouts  66.5 us (10%)
  matrix products  35 us (5%)
  other arithmetic  30 us (5%)
  between operations  15.2 us (2%)
    unnamed x12, waiting for transfers between devices  190 us
    reduce_scatter x1, waiting for transfers between devices, shards(): lax.psum_scatter(jnp.dot(inner, w_down, preferred_element_type=f32).resha...  59.1 us
    pmax x1, blocking collectives, shards(): top_all = lax.pmax(jnp.stack(shaped_all), ('seq', 'head'))  40.5 us
    all_gather x1, waiting for transfers between devices, project_tokens(): both = lax.all_gather(jnp.concatenate([q_raw, kv_raw], 1), 'seq', axis=1)  34.7 us
    psum x1, waiting for transfers between devices, shards(): lax.psum((gate_part, up_part, jnp.sum(state_f * state_f, -1)), 'head')  31.1 us
    all_gather x1, blocking collectives, shards(): result = lax.all_gather(result, 'seq', axis=0, tiled=True)  21.3 us
    all_gather x1, blocking collectives, shards(): state_all = lax.all_gather(state, 'seq', axis=0, tiled=True)  21.2 us
    all_gather x1, waiting for transfers between devices, shards(): lax.all_gather(w_keyval, 'seq', axis=1, tiled=True)  20.5 us
  transfers between devices with their start and end apart: 10, of which 10 were waited for; matrix products, arithmetic and copies ran while one was open for 11% of the time, Pallas kernels for 0%

commit v1 on v0

--- a/solution.py
+++ b/solution.py
@@ -220,7 +220,12 @@
     x_all = step_tokens.reshape(rows, -1)
     x_f = lax.dynamic_slice_in_dim(x_all, seq_at * per_dev, per_dev, 0).astype(f32)
     state = (x_f + out_proj * lax.rsqrt(out_sq / D + EPS)[:, None] * post_gain).astype(bf16)
-    state_all = lax.all_gather(state, "seq", axis=0, tiled=True)
+    ring = [state]
+    for hop in range(15):
+        ring.append(lax.ppermute(ring[-1], "seq", [(dev, (dev + 1) % 16) for dev in range(16)]))
+    state_all = jnp.roll(
+        jnp.concatenate(ring[::-1], axis=0), (lax.axis_index("seq") + 1) * ring[0].shape[0], axis=0
+    )
     state_f = state_all.astype(f32)
     scaled_two = (state_f * ffn_gain).astype(bf16)
     gate_part = jnp.dot(scaled_two, w_gate, preferred_element_type=f32)

time: 639 us -> 722 us (1.13); the launches traced: 638 us -> 712 us
  waiting for transfers between devices: 387 us -> 478 us
  blocking collectives: 104 us -> 82.4 us
    ppermute x0 -> x15, waiting for transfers between devices: none -> 91.8 us  [shards(): lax.ppermute(ring[-1], 'seq', [(dev, (dev + 1) % 16) for dev in range(16)])]
    all_gather x1 -> x0, blocking collectives: 21.2 us -> none  [shards(): state_all = lax.all_gather(state, 'seq', axis=0, tiled=True)]
  transfers between devices with their start and end apart: 10 -> 25, of which waited for: 10 -> 25; matrix products, arithmetic and copies ran while one was open for 11% -> 10% of each run, Pallas kernels for 0% -> 0%
where the time goes in v1:
time: 722 us; the launch traced here: 712 us
  waiting for transfers between devices  478 us (66%)
  blocking collectives  82.4 us (11%)
  local copies, waits for them, and re-layouts  70 us (10%)
  matrix products  35.1 us (5%)
  other arithmetic  30.5 us (4%)
  between operations  15.5 us (2%)
    unnamed x12, waiting for transfers between devices  190 us
    ppermute x15, waiting for transfers between devices, shards(): lax.ppermute(ring[-1], 'seq', [(dev, (dev + 1) % 16) for dev in range(16)])  91.8 us
    reduce_scatter x1, waiting for transfers between devices, shards(): lax.psum_scatter(jnp.dot(inner, w_down, preferred_element_type=f32).resha...  59.1 us
    pmax x1, blocking collectives, shards(): top_all = lax.pmax(jnp.stack(shaped_all), ('seq', 'head'))  40.4 us
    all_gather x1, waiting for transfers between devices, project_tokens(): both = lax.all_gather(jnp.concatenate([q_raw, kv_raw], 1), 'seq', axis=1)  34.7 us
    psum x1, waiting for transfers between devices, shards(): lax.psum((gate_part, up_part, jnp.sum(state_f * state_f, -1)), 'head')  30.9 us
    all_gather x1, blocking collectives, shards(): result = lax.all_gather(result, 'seq', axis=0, tiled=True)  21.3 us
    psum x1, waiting for transfers between devices, shards(): packed = lax.psum(packed, 'head')  20.5 us
  transfers between devices with their start and end apart: 25, of which 25 were waited for; matrix products, arithmetic and copies ran while one was open for 10% of the time, Pallas kernels for 0%

profile of v1, /device:TPU:0, one launch (start us, length us, event | category | flops | bytes accessed | tf_op | source)
XLA Modules:
  0.0 711.8 jit_solution(14731672712614422369)
XLA Ops:
  6.6 2.2 fusion.30
  8.8 2.1 fusion.29
  12.3 5.8 all-reduce.4
  18.1 18.1 %all-reduce.21.cloned.1.call-done = (f32[192,128]{1,0:T(8,128)}, f32[192,128]{1,0:T(8,128)}) async-done(((f32[192,128]{1,0:T(8,128)}, f32[192,128]{1,0:T(8,128)}), (f32[192,128]{1,0:T(8,128)}, f32[192,128]{1,0:T(8,128)})) %all-reduce.21.cloned.1.call-update) | async-done | bytes 196624 | tf_op jit(solution)/shard_map/psum | solution.py:41
  47.3 2.8 fusion.115
  50.1 2.7 reshape.490
  58.9 6.1 all-gather.8.cloned.1.call-done
  65.0 4.0 gather_fusion.8
  69.0 2.5 gather_fusion.3
  71.5 34.7 %all-gather.10.cloned.1.call-done = bf16[192,4096]{1,0:T(8,128)(2,1)} async-done(((bf16[192,256]{1,0:T(8,128)(2,1)}), bf16[192,4096]{1,0:T(8,128)(2,1)}) %all-gather.10.cloned.1.call-update) | async-done | bytes 1572880 | tf_op jit(solution)/shard_map/all_gather | solution.py:46
  106.2 1.8 copy.317
  122.1 2.7 select_select_fusion.1
  135.2 3.0 fusion.40
  138.2 2.9 copy.257
  146.3 20.3 %all-gather.6.cloned.1.call-done = bf16[1280,2048]{1,0:T(8,128)(2,1)} async-done(((bf16[1280,128]{1,0:T(8,128)(2,1)}), bf16[1280,2048]{1,0:T(8,128)(2,1)}) %all-gather.6.cloned.1.call-update) | async-done | bytes 5242896 | tf_op jit(solution)/shard_map/all_gather | solution.py:91
  166.6 4.2 fusion.127
  174.7 6.2 reduce-scatter.4.cloned.1.call-done
  185.6 40.4 %pmax.7 = f32[2,12,8,4,2]{2,4,3,1,0:T(2,128)S(1)} all-reduce(f32[2,12,8,4,2]{2,4,3,1,0:T(2,128)S(1)} %pad_maximum_fusion.2), channel_id=1, replica_groups=mesh['seq'=16,'head'=2] {'seq','head'}, use_global_device_ids=true, to_apply=%region_17.21 | all-reduce | flops 1536 | bytes 12288 | tf_op jit(solution)/shard_map/pmax | solution.py:157
  230.8 2.4 convolution_bitcast_fusion.2
  241.9 1.9 copy.263
  254.7 94.8 %all-reduce.15.cloned.1.call-done = f32[16,24832]{1,0:T(8,128)} async-done(((f32[16,24832]{1,0:T(8,128)}), f32[16,24832]{1,0:T(8,128)}) %all-reduce.15.cloned.1.call-update) | async-done | bytes 1589264
  349.5 2.5 constant_dynamic-slice_fusion.2
  352.1 20.5 %all-reduce.13.cloned.1.call-done = f32[1,24832]{1,0:T(1,128)} async-done(((f32[1,24832]{1,0:T(1,128)}), f32[1,24832]{1,0:T(1,128)}) %all-reduce.13.cloned.1.call-update) | async-done | bytes 99344 | tf_op jit(solution)/shard_map/psum | solution.py:210
  376.0 94.0 %all-reduce.17.cloned.1.call-done = f32[16,12,1280]{2,0,1:T(8,128)} async-done(((f32[16,12,1280]{2,0,1:T(8,128)}), f32[16,12,1280]{2,0,1:T(8,128)}) %all-reduce.17.cloned.1.call-update) | async-done | bytes 983056
  471.9 4.9 psum.67
  477.8 6.1 collective-permute-done
  483.9 6.1 collective-permute-done.1
  490.1 6.1 collective-permute-done.2
  496.2 6.1 collective-permute-done.3
  502.3 6.1 collective-permute-done.4
  508.4 6.1 collective-permute-done.5
  514.6 6.1 collective-permute-done.6
  520.7 6.1 collective-permute-done.7
  526.8 6.1 collective-permute-done.8
  532.9 6.1 collective-permute-done.9
  539.0 6.1 collective-permute-done.10
  545.2 6.1 collective-permute-done.11
  551.3 6.1 collective-permute-done.12
  557.4 6.1 collective-permute-done.13
  563.5 6.1 collective-permute-done.14
  569.7 3.1 concatenate.96
  572.8 2.9 fusion.44
  577.5 5.0 psum.69
  582.4 30.9 %all-reduce.19.cloned.1.call-done = (f32[192,640]{1,0:T(8,128)}, f32[192,640]{1,0:T(8,128)}) async-done(((f32[192,640]{1,0:T(8,128)}, f32[192,640]{1,0:T(8,128)}), (f32[192,640]{1,0:T(8,128)}, f32[192,640]{1,0:T(8,128)})) %all-reduce.19.cloned.1.call-update) | async-done | bytes 983056 | tf_op jit(solution)/shard_map/psum | solution.py:233
  613.4 1.9 fusion.50
  616.5 59.1 %reduce-scatter.6.cloned.1.call-done = f32[1,12,1280]{2,1,0:T(8,128)} async-done(((f32[16,12,1280]{2,1,0:T(8,128)}), f32[1,12,1280]{2,1,0:T(8,128)}) %reduce-scatter.6.cloned.1.call-update) | async-done | bytes 61456 | tf_op jit(solution)/shard_map/reduce_scatter | solution.py:238
  676.6 4.9 psum.71
  682.6 21.3 %all-gather.1 = bf16[16,12,1280]{2,1,0:T(8,128)(2,1)S(1)} all-gather(bf16[1,12,1280]{2,1,0:T(8,128)(2,1)S(1)} %fusion.87), channel_id=1, replica_groups=mesh['seq'=16,'head'=2] {'seq'}, dimensions={0}, use_global_device_ids=true | all-gather | bytes 522240 | tf_op jit(solution)/shard_map/all_gather | solution.py:248
  (316 shorter events, 91.9 us)
Async XLA Ops:
  6.5 606.8 %copy-start = (bf16[640,1280]{1,0:T(8,128)(2,1)S(1)}, bf16[640,1280]{1,0:T(8,128)(2,1)}, u32[]{:S(2)}) copy-start(bf16[640,1280]{1,0:T(8,128)(2,1)} %param.44) | copy-start | bytes 4915204
  6.5 29.7 %all-reduce.21.cloned.1.call-start = ((), (), s32[]{:S(2)}) async-start(), calls=%async_computation.11 | async-start | bytes 393216 | tf_op jit(solution)/shard_map/psum | solution.py:41
  10.8 27.7 %copy-start.42 = (f32[256]{0:T(256)S(1)}, f32[256]{0:T(256)}, u32[]{:S(2)}) copy-start(f32[256]{0:T(256)} %param.38) | copy-start | bytes 3076
  10.9 27.8 %copy-start.45 = (s32[12]{0:T(128)S(1)}, s32[12]{0:T(128)}, u32[]{:S(2)}) copy-start(s32[12]{0:T(128)} %param.29) | copy-start | bytes 148
  10.9 28.6 %copy-start.43 = (f32[256]{0:T(256)S(1)}, f32[256]{0:T(256)}, u32[]{:S(2)}) copy-start(f32[256]{0:T(256)} %param.37) | copy-start | bytes 3076
  10.9 28.6 %copy-start.34 = (s32[2,12,8]{1,2,0:T(8,128)S(1)}, s32[2,12,8]{1,2,0:T(8,128)}, u32[]{:S(2)}) copy-start(s32[2,12,8]{1,2,0:T(8,128)} %param.27) | copy-start | bytes 2308
  10.9 54.1 %all-gather.8.cloned.1.call-start = ((), (), s32[]{:S(2)}) async-start(), calls=%async_computation.4 | async-start | bytes 2359296 | tf_op jit(solution)/shard_map/all_gather | solution.py:115
  11.6 94.5 %all-gather.10.cloned.1.call-start = ((), (), s32[]{:S(2)}) async-start(), calls=%async_computation.7 | async-start | bytes 1671168 | tf_op jit(solution)/shard_map/all_gather | solution.py:46
  37.9 128.6 %all-gather.6.cloned.1.call-start = ((), (), s32[]{:S(2)}) async-start(), calls=%async_computation.2 | async-start | bytes 5570560 | tf_op jit(solution)/shard_map/all_gather | solution.py:91
  38.5 142.3 %reduce-scatter.4.cloned.1.call-start = ((), (), s32[]{:S(2)}) async-start(), calls=%async_computation.3 | async-start | bytes 393216 | tf_op jit(solution)/shard_map/reduce_scatter | solution.py:95
  38.6 75.7 %copy-start.31 = (f32[1,2,4,128]{3,1,2,0:T(2,128)}, f32[1,2,4,128]{3,1,2,0:T(2,128)S(1)}, u32[]{:S(2)}) copy-start(f32[1,2,4,128]{3,1,2,0:T(2,128)S(1)} %copy.316) | copy-start | bytes 12292
  58.9 82.1 %copy-start.23 = (pred[12,8,4,4]{0,1,3,2:T(8,128)(4,1)}, pred[12,8,4,4]{0,1,3,2:T(8,128)(4,1)S(1)}, u32[]{:S(2)}) copy-start(pred[12,8,4,4]{0,1,3,2:T(8,128)(4,1)S(1)} %get-tuple-element.66) | copy-start | bytes 4612
  142.8 23.7 %copy-start.20 = (bf16[32,1280]{1,0:T(8,128)(2,1)S(1)}, bf16[32,1280]{1,0:T(8,128)(2,1)}, u32[]{:S(2)}) copy-start(bf16[32,1280]{1,0:T(8,128)(2,1)} %reshape.483) | copy-start | bytes 245764
  146.3 24.6 %copy-start.4 = (f32[12,4,4,4,8,2]{0,4,3,2,5,1:T(8,128)S(1)}, f32[12,4,4,4,8,2]{0,4,3,2,5,1:T(8,128)}, u32[]{:S(2)}) copy-start(f32[12,4,4,4,8,2]{0,4,3,2,5,1:T(8,128)} %copy.241) | copy-start | bytes 147460
  146.3 24.6 %copy-start.25 = (pred[12,8,4,4]{0,1,3,2:T(8,128)(4,1)S(1)}, pred[12,8,4,4]{0,1,3,2:T(8,128)(4,1)}, u32[]{:S(2)}) copy-start(pred[12,8,4,4]{0,1,3,2:T(8,128)(4,1)} %get-tuple-element.65) | copy-start | bytes 4612
  146.3 24.7 %copy-start.10 = (bf16[12,4,4,1024]{3,2,1,0:T(4,128)(2,1)S(1)}, bf16[12,4,4,1024]{3,2,1,0:T(4,128)(2,1)}, u32[]{:S(2)}) copy-start(bf16[12,4,4,1024]{3,2,1,0:T(4,128)(2,1)} %get-tuple-element.26) | copy-start | bytes 1179652
  170.8 10.0 %copy-start.44 = (f32[16]{0:T(128)S(1)}, f32[16]{0:T(128)}, u32[]{:S(2)}) copy-start(f32[16]{0:T(128)} %fusion.105) | copy-start | bytes 196
  170.8 178.7 %all-reduce.15.cloned.1.call-start = ((), (), s32[]{:S(2)}) async-start(), calls=%async_computation.8 | async-start | bytes 3178496
  170.9 11.2 %copy-start.32 = (f32[1,2,4,128]{3,1,2,0:T(2,128)S(1)}, f32[1,2,4,128]{3,1,2,0:T(2,128)}, u32[]{:S(2)}) copy-start(f32[1,2,4,128]{3,1,2,0:T(2,128)} %copy-done.31) | copy-start | bytes 12292
  171.9 10.4 %copy-start.41 = (pred[4,4]{1,0:T(4,128)(4,1)S(1)}, pred[4,4]{1,0:T(4,128)(4,1)}, u32[]{:S(2)}) copy-start(pred[4,4]{1,0:T(4,128)(4,1)} %broadcast_compare_fusion.1) | copy-start | bytes 52
  173.0 11.7 %copy-start.28 = (f32[8,8,4,2]{1,3,2,0:T(2,128)S(1)}, f32[8,8,4,2]{1,3,2,0:T(2,128)}, u32[]{:S(2)}) copy-start(f32[8,8,4,2]{1,3,2,0:T(2,128)} %get-tuple-element.67) | copy-start | bytes 6148
  174.6 9.0 %copy-start.29 = (bf16[32,2048]{1,0:T(8,128)(2,1)S(1)}, bf16[32,2048]{1,0:T(8,128)(2,1)}, u32[]{:S(2)}) copy-start(bf16[32,2048]{1,0:T(8,128)(2,1)} %get-tuple-element.33) | copy-start | bytes 393220
  174.6 10.1 %copy-start.21 = (f32[12,8,4,2]{1,3,2,0:T(2,128)S(1)}, f32[12,8,4,2]{1,3,2,0:T(2,128)}, u32[]{:S(2)}) copy-start(f32[12,8,4,2]{1,3,2,0:T(2,128)} %copy.258) | copy-start | bytes 9220
  182.2 48.7 %copy-start.14 = (f32[8,8,4,2,64]{4,1,3,2,0:T(8,128)S(1)}, f32[8,8,4,2,64]{4,1,3,2,0:T(8,128)}, u32[]{:S(2)}) copy-start(f32[8,8,4,2,64]{4,1,3,2,0:T(8,128)} %get-tuple-element.68) | copy-start | bytes 393220
  226.7 6.5 copy-start.36
  253.4 121.2 %copy-start.19 = (bf16[128,1280]{1,0:T(8,128)(2,1)S(1)}, bf16[128,1280]{1,0:T(8,128)(2,1)}, u32[]{:S(2)}) copy-start(bf16[128,1280]{1,0:T(8,128)(2,1)} %param.39) | copy-start | bytes 983044
  253.4 119.2 %all-reduce.13.cloned.1.call-start = ((), (), s32[]{:S(2)}) async-start(), calls=%async_computation.5 | async-start | bytes 198656 | tf_op jit(solution)/shard_map/psum | solution.py:210
  352.1 117.9 %all-reduce.17.cloned.1.call-start = ((), (), s32[]{:S(2)}) async-start(), calls=%async_computation.9 | async-start | bytes 1966080
  373.3 103.5 %copy-start.39 = (f32[1280]{0:T(1024)S(1)}, f32[1280]{0:T(1024)}, u32[]{:S(2)}) copy-start(f32[1280]{0:T(1024)} %param.40) | copy-start | bytes 15364
  375.9 196.9 %copy-start.33 = (f32[1280]{0:T(1024)S(1)}, f32[1280]{0:T(1024)}, u32[]{:S(2)}) copy-start(f32[1280]{0:T(1024)} %param.41) | copy-start | bytes 15364
  375.9 237.5 %all-reduce.19.cloned.1.call-start = ((), (), s32[]{:S(2)}) async-start(), calls=%async_computation.10 | async-start | bytes 1966080 | tf_op jit(solution)/shard_map/psum | solution.py:233
  477.7 6.2 collective-permute-start
  483.9 6.1 collective-permute-start.1
  490.0 6.1 collective-permute-start.2
  496.2 6.1 collective-permute-start.3
  502.3 6.1 collective-permute-start.4
  508.4 6.1 collective-permute-start.5
  514.5 6.1 collective-permute-start.6
  520.7 6.1 collective-permute-start.7
  526.8 6.1 collective-permute-start.8
  532.9 6.1 collective-permute-start.9
  539.0 6.1 collective-permute-start.10
  545.2 6.1 collective-permute-start.11
  551.3 6.1 collective-permute-start.12
  557.4 6.1 collective-permute-start.13
  563.5 6.1 collective-permute-start.14
  577.2 98.5 %reduce-scatter.6.cloned.1.call-start = ((), (), s32[]{:S(2)}) async-start(), calls=%async_computation.6 | async-start | bytes 1392640 | tf_op jit(solution)/shard_map/reduce_scatter | solution.py:238
  615.3 66.3 %copy-start.40 = (f32[1280]{0:T(1024)S(1)}, f32[1280]{0:T(1024)}, u32[]{:S(2)}) copy-start(f32[1280]{0:T(1024)} %param.45) | copy-start | bytes 15364
  (27 other events, 87.0 us)
Sparse Core Ops, SparseCore 0:
  11.0 25.1 all-reduce.20
  37.7 27.2 all-gather.7
  67.2 38.9 all-gather.9
  108.2 58.3 all-gather.5
  170.9 9.8 reduce-scatter.3
  253.5 95.9 all-reduce.14
  352.2 20.3 all-reduce.12
  376.0 93.9 all-reduce.16
  577.3 36.0 all-reduce.18
  617.3 58.2 reduce-scatter.5
